TPU v7x, 128 devices: a whole 4x4x4 slice. The times are simulated.
128 devices in a mesh: dp: 4 (over y_hi, core), head: 4 (over x), ctx: 8 (over z, y_lo).
Axes of the slice: x: 4, y: 4 (y_hi: 2, y_lo: 2; y = y_hi * 2 + y_lo), z: 4, core: 2. Of those that a mesh axis runs over, the one named last changes fastest.
Arguments:
- video: bfloat16 [16, 64, 24576], P('dp', 'head', 'ctx'), parts along dimension 0, may hold values from -6 to 6
- cache: bfloat16 [8, 64, 24576], P('dp', 'head', 'ctx'), parts along dimension 0, may hold values from -6 to 6
- conv_weight: bfloat16 [3, 3, 288, 192], replicated, may hold values from -0.125 to 0.125
- conv_bias: float32 [192], replicated, may hold values from -3 to 3
- down_weight: bfloat16 [768, 192], replicated, may hold values from -0.21875 to 0.21875
- patch_weight: bfloat16 [768, 5120], P(None, ('head', 'ctx')), may hold values from -0.21875 to 0.21875
- step_index: int32 [4], P('dp'), parts along dimension 0, may hold values from 0 to 999
- mod_weight: bfloat16 [256, 10240], P(None, ('head', 'ctx')), may hold values from -1 to 1
- qkv_weight: bfloat16 [5120, 20, 3, 128], P('ctx', 'head'), may hold values from -0.078125 to 0.078125
Outputs:
- attended: bfloat16 [16384, 2560], P(('dp', 'ctx'), 'head'), parts along dimension 0
There are 4 independent parts, one for each index of `dp`. A program takes and returns all parts, laid end to end along the dimension named above; an argument that names none is the same for every part. Nothing has to cross between parts.
All inputs are finite; a program needn't handle non-finite values.
Results may differ from a plain program's by a relative error of at most 0.015.
The roundings to bfloat16 on the way count: a program that leaves them out, or rounds other values in their place, can miss the bound.
Values may be sent and summed in bfloat16 or wider, within the bound.
No kernel may reach another device: no remote copies, remote signals or barrier semaphores. Data moves between devices by JAX's collectives and lax.ppermute only.
A program may use at most 128 MiB of HBM per device.

v0:
```python
import jax
import jax.numpy as jnp
from jax import lax
from jax.sharding import PartitionSpec as P

D = 5120
HDIM = 128
FREQ = 256


def with_halo(cells, sides, width):
    for axis, dim in sides:
        count = lax.axis_size(axis)
        ends = count - 1
        head = lax.slice_in_dim(cells, 0, width, axis=dim)
        tail = lax.slice_in_dim(cells, cells.shape[dim] - width, cells.shape[dim], axis=dim)
        cells = jnp.concatenate(
            [
                lax.ppermute(tail, axis, [(i, (i + 1) % count) for i in range(ends)]),
                cells,
                lax.ppermute(head, axis, [((i + 1) % count, i) for i in range(ends)]),
            ],
            axis=dim,
        )
    return cells


def silu_act(value):
    return value * jax.nn.sigmoid(value)


def shards(
    video,
    cache,
    conv_weight,
    conv_bias,
    down_weight,
    patch_weight,
    step_index,
    mod_weight,
    qkv_weight,
):
    cin = conv_weight.shape[2] // 3
    cmid = conv_weight.shape[3]
    frame_count = video.shape[0]
    tile_rows = video.shape[1]
    tile_cols = video.shape[2] // cin
    frames = jnp.concatenate([cache, video], 0).reshape(frame_count + 2, tile_rows, tile_cols, cin)
    padded = with_halo(frames, (("head", 1), ("ctx", 2)), 1)
    total = jnp.zeros((frame_count, tile_rows, tile_cols, cmid), jnp.float32)
    for time_tap in range(3):
        for row_tap in range(3):
            slab = padded[time_tap : time_tap + frame_count, row_tap : row_tap + tile_rows]
            stacked = jnp.concatenate(
                [slab[:, :, col_tap : col_tap + tile_cols] for col_tap in range(3)], -1
            )
            total = total + jnp.einsum(
                "fyxc,cd->fyxd",
                stacked,
                conv_weight[time_tap, row_tap],
                preferred_element_type=jnp.float32,
            )
    hidden = silu_act(total + conv_bias).astype(jnp.bfloat16)
    stacked = (
        hidden.reshape(frame_count, tile_rows // 2, 2, tile_cols // 2, 2, cmid)
        .transpose(0, 1, 3, 2, 4, 5)
        .reshape(-1, 4 * cmid)
    )
    reduced = silu_act(jnp.dot(stacked, down_weight, preferred_element_type=jnp.float32)).astype(
        jnp.bfloat16
    )
    reduced = reduced.reshape(frame_count, tile_rows // 2, tile_cols // 2, cmid)
    patches = reduced.reshape(frame_count, tile_rows // 4, 2, tile_cols // 4, 2, cmid).transpose(
        0, 1, 3, 2, 4, 5
    )
    patches = patches.reshape(-1, 4 * cmid)
    half = FREQ // 2
    freqs = jnp.exp(-jnp.log(10000.0) * jnp.arange(half, dtype=jnp.float32) / half)
    angles = step_index[0].astype(jnp.float32) * freqs
    timing = jnp.concatenate([jnp.cos(angles), jnp.sin(angles)]).astype(jnp.bfloat16)
    mod_share = jnp.dot(timing[None, :], mod_weight, preferred_element_type=jnp.float32)[0]
    modulation = lax.all_gather(mod_share, ("head", "ctx"), axis=0, tiled=True)
    scale = modulation[:D]
    shift = modulation[D:]
    embedded = jnp.dot(
        patches,
        lax.all_gather(patch_weight, ("head", "ctx"), axis=1, tiled=True),
        preferred_element_type=jnp.float32,
    )
    inverse = lax.rsqrt(jnp.mean(embedded * embedded, -1, keepdims=True) + 1e-06)
    normed = (embedded * inverse * (1.0 + scale) + shift).astype(jnp.bfloat16)
    gathered = lax.all_gather(normed, "head", axis=0, tiled=True)
    group_rows = gathered.shape[0]
    heads_here = qkv_weight.shape[1]
    out_cols = heads_here * 3 * HDIM
    piece = lax.all_gather(qkv_weight, "ctx", axis=0, tiled=True)
    qkv = jnp.dot(
        gathered, piece.reshape(piece.shape[0], out_cols), preferred_element_type=jnp.float32
    )
    qkv = qkv.astype(jnp.bfloat16).reshape(group_rows, heads_here, 3, HDIM)
    query = qkv[:, :, 0]
    keys = qkv[:, :, 1]
    values = qkv[:, :, 2]
    inv_root = 1.0 / jnp.sqrt(jnp.float32(HDIM))
    best = jnp.full((heads_here, group_rows), -1e30, jnp.float32)
    key_piece = lax.all_gather(keys, "ctx", axis=0, tiled=True)
    value_piece = lax.all_gather(values, "ctx", axis=0, tiled=True)
    scores = (
        jnp.einsum("qhd,khd->hqk", query, key_piece, preferred_element_type=jnp.float32) * inv_root
    )
    new_best = jnp.maximum(best, jnp.max(scores, -1))
    probs = jnp.exp(scores - new_best[..., None])
    denom = jnp.sum(probs, -1)
    accum = jnp.einsum(
        "hqk,khd->hqd", probs.astype(jnp.bfloat16), value_piece, preferred_element_type=jnp.float32
    )
    best, denom, accum = (new_best, denom, accum)
    result = (accum / denom[..., None]).astype(jnp.bfloat16)
    return result.transpose(1, 0, 2).reshape(group_rows, heads_here * HDIM)


def solution(mesh):
    return jax.shard_map(
        shards,
        mesh=mesh,
        in_specs=(
            P("dp", "head", "ctx"),
            P("dp", "head", "ctx"),
            P(),
            P(),
            P(),
            P(None, ("head", "ctx")),
            P("dp"),
            P(None, ("head", "ctx")),
            P("ctx", "head", None, None),
        ),
        out_specs=P(("dp", "ctx"), "head"),
        check_vma=False,
    )
```

profile of v0, /device:TPU:1, one launch (start us, length us, event | category | flops | bytes accessed | tf_op | source)
XLA Modules:
  0.0 923.7 jit_solution(17581543572212077937)
XLA Ops:
  10.8 4.6 collective-permute-start
  15.3 1.3 collective-permute-start.1
  19.2 141.1 %all-reduce = f32[10240]{0:T(1024)S(1)} all-reduce(f32[10240]{0:T(1024)S(1)} %dynamic-update-slice), channel_id=1, replica_groups=mesh['dp'=4,'head'=4,'ctx'=8] {'head','ctx'}, use_global_device_ids=true, to_apply=%add | all-reduce | flops 10240 | bytes 81920
  164.3 1.3 collective-permute-start.2
  165.6 1.5 collective-permute-start.3
  167.6 1.4 collective-permute-done.2
  168.9 1.9 fusion.81
  170.8 1.3 collective-permute-done.3
  172.1 2.1 fusion.73
  181.5 2.6 multiply_convert_fusion
  187.7 8.9 all-gather.8.cloned.1.call-done
  196.7 5.9 multiply_reduce_fusion.1
  202.6 1.5 add_convert_fusion
  204.8 3.1 copy.17
  208.0 63.2 %all-gather.10.cloned.1.call-done = bf16[512,5120]{1,0:T(8,128)(2,1)} async-done(((bf16[128,5120]{1,0:T(8,128)(2,1)}), bf16[512,5120]{1,0:T(8,128)(2,1)}) %all-gather.10.cloned.1.call-update) | async-done | bytes 5242896 | tf_op jit(solution)/shard_map/all_gather | solution.py:92
  271.2 381.9 %all-gather.12.cloned.1.call-done = bf16[5120,5,3,128]{0,3,2,1:T(8,128)(2,1)} async-done(((bf16[640,5,3,128]{0,3,2,1:T(8,128)(2,1)}), bf16[5120,5,3,128]{0,3,2,1:T(8,128)(2,1)}) %all-gather.12.cloned.1.call-update) | async-done | bytes 19660816 | tf_op jit(solution)/shard_map/all_gather | solution.py:96
  653.1 17.7 %convolution_convert_fusion = bf16[512,1920]{1,0:T(8,128)(2,1)} fusion(bf16[512,5120]{1,0:T(8,128)(2,1)} %all-gather.10.cloned.1.call-done, bf16[5120,1920]{0,1:T(8,128)(2,1)} %bitcast.113), kind=kOutput, calls=%fused_computation.24 | convolution fusion | flops 10067312640 | bytes 26869760 | tf_op jit(solution)/shard_map/dot_general | solution.py:97
  670.8 2.7 copy.18
  674.5 1.1 copy.33
  676.2 110.6 %all-gather.14.cloned.1.call-done = bf16[4096,5,1,128]{3,0,1,2:T(8,128)(2,1)} async-done(((bf16[512,5,1,128]{3,0,1,2:T(8,128)(2,1)}), bf16[4096,5,1,128]{3,0,1,2:T(8,128)(2,1)}) %all-gather.14.cloned.1.call-update) | async-done | bytes 5242896 | tf_op jit(solution)/shard_map/all_gather | solution.py:106
  786.8 19.0 %multiply_reduce_fusion = (f32[5,512]{1,0:T(8,128)S(1)}, f32[5,512,4096]{2,1,0:T(8,128)}) fusion(bf16[4096,5,1,128]{3,0,1,2:T(8,128)(2,1)} %all-gather.14.cloned.1.call-done, bf16[512,5,3,128]{0,3,2,1:T(8,128)(2,1)S(1)} %bitcast.108), kind=kOutput, calls=%fused_computation.1 | convolution fusion | flops 2705323520 | bytes 47851520 | tf_op jit(solution)/shard_map/qhd,khd->hqk/dot_general | solution.py:109
  805.8 17.3 %fusion = f32[5,512]{1,0:T(8,128)S(1)} fusion(f32[5,512,4096]{2,1,0:T(8,128)} %get-tuple-element.47, f32[5,512]{1,0:T(8,128)S(1)} %broadcast_maximum_fusion), kind=kLoop, calls=%fused_computation.2 | loop fusion | flops 31454720 | bytes 41963520 | tf_op jit(solution)/shard_map/reduce_sum | solution.py:113
  823.2 75.6 %all-gather.16.cloned.1.call-done = bf16[4096,5,1,128]{0,3,1,2:T(8,128)(2,1)} async-done(((bf16[512,5,1,128]{0,3,1,2:T(8,128)(2,1)}), bf16[4096,5,1,128]{0,3,1,2:T(8,128)(2,1)}) %all-gather.16.cloned.1.call-update) | async-done | bytes 5242896 | tf_op jit(solution)/shard_map/all_gather | solution.py:107
  898.7 17.3 %divide_convert_fusion = bf16[512,5,128]{0,2,1:T(8,128)(2,1)S(1)} fusion(bf16[4096,5,1,128]{0,3,1,2:T(8,128)(2,1)} %all-gather.16.cloned.1.call-done, f32[5,512,4096]{2,1,0:T(8,128)} %get-tuple-element.47, f32[5,512]{1,0:T(8,128)S(1)} %broadcast_maximum_fusion, f32[512,5]{0,1:T(8,128)S(1)} %bitcast.112), kind=kOutput, calls=%fused_computation.84 | convolution fusion | flops 2716467200 | bytes 47861760 | tf_op jit(solution)/shard_map/hqk,khd->hqd/dot_general | solution.py:114
  (70 shorter events, 23.9 us)
Async XLA Ops:
  6.5 180.0 %copy-start = (bf16[768,192]{0,1:T(8,128)(2,1)S(1)}, bf16[768,192]{0,1:T(8,128)(2,1)}, u32[]{:S(2)}) copy-start(bf16[768,192]{0,1:T(8,128)(2,1)} %param.13) | copy-start | bytes 884740
  6.5 10.8 %copy-start.7 = (u32[128]{0:T(128)S(1)}, u32[128]{0:T(128)}, u32[]{:S(2)}) copy-start(u32[128]{0:T(128)} %constant.27) | copy-start | bytes 1540
  6.5 12.2 %copy-start.4 = (bf16[256,320]{0,1:T(8,128)(2,1)S(1)}, bf16[256,320]{0,1:T(8,128)(2,1)}, u32[]{:S(2)}) copy-start(bf16[256,320]{0,1:T(8,128)(2,1)} %param.16) | copy-start | bytes 491524
  6.5 190.1 %all-gather.8.cloned.1.call-start = ((), (), s32[]{:S(2)}) async-start(), calls=%async_computation | async-start | bytes 8110080 | tf_op jit(solution)/shard_map/all_gather | solution.py:87
  7.3 264.0 %all-gather.10.cloned.1.call-start = ((), (), s32[]{:S(2)}) async-start(), calls=%async_computation.1 | async-start | bytes 6553600 | tf_op jit(solution)/shard_map/all_gather | solution.py:92
  8.3 152.2 %copy-start.3 = (bf16[4,16,3072]{2,1,0:T(8,128)(2,1)S(1)}, bf16[4,16,3072]{2,1,0:T(8,128)(2,1)}, u32[]{:S(2)}) copy-start(bf16[4,16,3072]{2,1,0:T(8,128)(2,1)} %param.9) | copy-start | bytes 1179652
  10.8 151.3 %collective-permute-start = (bf16[6,1,32,96]{3,2,1,0:T(8,128)(2,1)}, bf16[6,1,32,96]{3,2,1,0:T(8,128)(2,1)}, u32[]{:S(2)}, u32[]{:S(2)}) collective-permute-start(bf16[6,1,32,96]{3,2,1,0:T(8,128)(2,1)} %get-tuple-element.35), channel_id=1, source_target_pairs={{0,8},{8,16},{16,24},{1,9},{9,17},{17,25},{2,10},{10,18},{18,26},{... | collective-permute-start | bytes 110600 | tf_op jit(solution)/shard_map/ppermute | solution.py:19
  15.3 148.0 %collective-permute-start.1 = (bf16[6,1,32,96]{3,2,1,0:T(8,128)(2,1)}, bf16[6,1,32,96]{3,2,1,0:T(8,128)(2,1)}, u32[]{:S(2)}, u32[]{:S(2)}) collective-permute-start(bf16[6,1,32,96]{3,2,1,0:T(8,128)(2,1)} %get-tuple-element.34), channel_id=1, source_target_pairs={{8,0},{16,8},{24,16},{9,1},{17,9},{25,17},{10,2},{18,10},{26,18},{... | collective-permute-start | bytes 110600 | tf_op jit(solution)/shard_map/ppermute | solution.py:21
  164.3 4.6 collective-permute-start.2
  165.6 6.5 collective-permute-start.3
  170.8 3.4 copy-start.5
  180.5 0.9 copy-start.6
  202.6 2.2 copy-start.2
  204.1 449.0 %all-gather.12.cloned.1.call-start = ((), (), s32[]{:S(2)}) async-start(), calls=%async_computation.2 | async-start | bytes 22118400 | tf_op jit(solution)/shard_map/all_gather | solution.py:96
  207.9 578.8 %all-gather.14.cloned.1.call-start = ((), (), s32[]{:S(2)}) async-start(), calls=%async_computation.3 | async-start | bytes 5898240 | tf_op jit(solution)/shard_map/all_gather | solution.py:106
  675.6 223.2 %all-gather.16.cloned.1.call-start = ((), (), s32[]{:S(2)}) async-start(), calls=%async_computation.4 | async-start | bytes 5898240 | tf_op jit(solution)/shard_map/all_gather | solution.py:107
  898.7 18.4 %copy-start.1 = (bf16[768,192]{0,1:T(8,128)(2,1)S(1)}, bf16[768,192]{0,1:T(8,128)(2,1)}, u32[]{:S(2)}) copy-start(bf16[768,192]{0,1:T(8,128)(2,1)} %param.13) | copy-start | bytes 884740
Sparse Core Ops, SparseCore 0:
  9.0 187.6 all-gather.7
  204.2 66.9 all-gather.9
  272.9 380.1 all-gather.11
  675.7 111.0 all-gather.13
  788.3 110.4 all-gather.15
where the time goes:
time: 924 us
  waiting for transfers between devices  644 us (70%)
  blocking collectives  141 us (15%)
  matrix products  70.4 us (8%)
  other arithmetic  22.9 us (2%)
  local copies, waits for them, and re-layouts  21.4 us (2%)
  between operations  14.9 us (2%)
    all_gather x1, waiting for transfers between devices, shards(): piece = lax.all_gather(qkv_weight, 'ctx', axis=0, tiled=True)  382 us
    unnamed x1, blocking collectives  141 us
    all_gather x1, waiting for transfers between devices, shards(): key_piece = lax.all_gather(keys, 'ctx', axis=0, tiled=True)  111 us
    all_gather x1, waiting for transfers between devices, shards(): value_piece = lax.all_gather(values, 'ctx', axis=0, tiled=True)  75.6 us
    all_gather x1, waiting for transfers between devices, shards(): gathered = lax.all_gather(normed, 'head', axis=0, tiled=True)  63.2 us
    dot_general x1, matrix products, shards(): jnp.einsum('qhd,khd->hqk', query, key_piece, preferred_element_type=jnp.f...  19 us
  transfers between devices with their start and end apart: 9, of which 7 were waited for; matrix products, arithmetic and copies ran while one was open for 7% of the time, Pallas kernels for 0%

commit v1 on v0

--- a/solution.py
+++ b/solution.py
@@ -103,7 +103,9 @@
     values = qkv[:, :, 2]
     inv_root = 1.0 / jnp.sqrt(jnp.float32(HDIM))
     best = jnp.full((heads_here, group_rows), -1e30, jnp.float32)
-    key_piece = lax.all_gather(keys, "ctx", axis=0, tiled=True)
+    key_piece = jnp.concatenate(
+        lax.all_to_all(jnp.stack([keys] * lax.axis_size("ctx")), "ctx", 0, 0), axis=0
+    )
     value_piece = lax.all_gather(values, "ctx", axis=0, tiled=True)
     scores = (
         jnp.einsum("qhd,khd->hqk", query, key_piece, preferred_element_type=jnp.float32) * inv_root

time: 924 us -> 868 us (0.939)
  waiting for transfers between devices: 644 us -> 466 us
  blocking collectives: 141 us -> 258 us
    all_to_all x0 -> x1, blocking collectives: none -> 118 us  [shards(): lax.all_to_all(jnp.stack([keys] * lax.axis_size('ctx')), 'ctx', 0, 0)]
    all_gather x1 -> x0, waiting for transfers between devices: 111 us -> none  [shards(): key_piece = lax.all_gather(keys, 'ctx', axis=0, tiled=True)]
    all_gather x1, waiting for transfers between devices: 75.6 us -> 5.96 us  [shards(): value_piece = lax.all_gather(values, 'ctx', axis=0, tiled=True)]
  transfers between devices with their start and end apart: 9 -> 8, of which waited for: 7 -> 6; matrix products, arithmetic and copies ran while one was open for 7% -> 8% of each run, Pallas kernels for 0% -> 0%
where the time goes in v1:
time: 868 us; the launch traced here: 867 us
  waiting for transfers between devices  466 us (54%)
  blocking collectives  258 us (30%)
  matrix products  70.5 us (8%)
  local copies, waits for them, and re-layouts  26.2 us (3%)
  other arithmetic  22.8 us (3%)
  between operations  14.8 us (2%)
  starting transfers between devices  8.72 us (1%)
    all_gather x1, waiting for transfers between devices, shards(): piece = lax.all_gather(qkv_weight, 'ctx', axis=0, tiled=True)  382 us
    unnamed x1, blocking collectives  140 us
    all_to_all x1, blocking collectives, shards(): lax.all_to_all(jnp.stack([keys] * lax.axis_size('ctx')), 'ctx', 0, 0)  118 us
    all_gather x1, waiting for transfers between devices, shards(): gathered = lax.all_gather(normed, 'head', axis=0, tiled=True)  64.5 us
    dot_general x1, matrix products, shards(): jnp.einsum('qhd,khd->hqk', query, key_piece, preferred_element_type=jnp.f...  19 us
    dot_general x1, matrix products, shards(): jnp.dot(gathered, piece.reshape(piece.shape[0], out_cols), preferred_elem...  17.7 us
    dot_general x1, matrix products, shards(): jnp.einsum('hqk,khd->hqd', probs.astype(jnp.bfloat16), value_piece, prefe...  17.4 us
  transfers between devices with their start and end apart: 8, of which 6 were waited for; matrix products, arithmetic and copies ran while one was open for 8% of the time, Pallas kernels for 0%

profile of v1, /device:TPU:1, one launch (start us, length us, event | category | flops | bytes accessed | tf_op | source)
XLA Modules:
  0.0 867.4 jit_solution(3521215572100933920)
XLA Ops:
  10.8 4.6 collective-permute-start
  15.3 1.3 collective-permute-start.1
  19.0 139.9 %all-reduce = f32[10240]{0:T(1024)S(1)} all-reduce(f32[10240]{0:T(1024)S(1)} %dynamic-update-slice), channel_id=1, replica_groups=mesh['dp'=4,'head'=4,'ctx'=8] {'head','ctx'}, use_global_device_ids=true, to_apply=%add | all-reduce | flops 10240 | bytes 81920
  162.9 1.3 collective-permute-start.2
  164.2 1.5 collective-permute-start.3
  166.2 1.5 collective-permute-done.2
  167.6 1.9 fusion.80
  170.7 2.1 fusion.72
  180.1 2.6 multiply_convert_fusion
  186.3 10.4 %all-gather.6.cloned.1.call-done = bf16[768,5120]{0,1:T(8,128)(2,1)} async-done(((bf16[768,160]{0,1:T(8,128)(2,1)}), bf16[768,5120]{0,1:T(8,128)(2,1)}) %all-gather.6.cloned.1.call-update) | async-done | bytes 7864336 | tf_op jit(solution)/shard_map/all_gather | solution.py:87
  196.7 5.9 multiply_reduce_fusion.1
  202.7 1.5 add_convert_fusion
  204.9 3.1 copy.26
  208.1 64.5 %all-gather.8.cloned.1.call-done = bf16[512,5120]{1,0:T(8,128)(2,1)} async-done(((bf16[128,5120]{1,0:T(8,128)(2,1)}), bf16[512,5120]{1,0:T(8,128)(2,1)}) %all-gather.8.cloned.1.call-update) | async-done | bytes 5242896 | tf_op jit(solution)/shard_map/all_gather | solution.py:92
  272.5 381.9 %all-gather.10.cloned.1.call-done = bf16[5120,5,3,128]{0,3,2,1:T(8,128)(2,1)} async-done(((bf16[640,5,3,128]{0,3,2,1:T(8,128)(2,1)}), bf16[5120,5,3,128]{0,3,2,1:T(8,128)(2,1)}) %all-gather.10.cloned.1.call-update) | async-done | bytes 19660816 | tf_op jit(solution)/shard_map/all_gather | solution.py:96
  654.4 17.7 %convolution_convert_fusion = bf16[512,1920]{1,0:T(8,128)(2,1)} fusion(bf16[512,5120]{1,0:T(8,128)(2,1)} %all-gather.8.cloned.1.call-done, bf16[5120,1920]{0,1:T(8,128)(2,1)} %bitcast.113), kind=kOutput, calls=%fused_computation.22 | convolution fusion | flops 10067312640 | bytes 26869760 | tf_op jit(solution)/shard_map/dot_general | solution.py:97
  672.2 2.7 copy.27
  676.9 2.3 stack.3
  679.2 118.3 %all_to_all.5 = bf16[8,512,5,128]{3,1,2,0:T(8,128)(2,1)S(1)} all-to-all(bf16[8,512,5,128]{3,1,2,0:T(8,128)(2,1)S(1)} %stack.3), channel_id=1, replica_groups=mesh['dp'=4,'head'=4,'ctx'=8] {'ctx'}, dimensions={0} | all-to-all | bytes 10485760 | tf_op jit(solution)/shard_map/all_to_all | solution.py:107
  797.5 2.6 copy.30
  800.1 19.0 %multiply_reduce_fusion = (f32[5,512]{1,0:T(8,128)S(1)}, f32[5,512,4096]{2,1,0:T(8,128)}) fusion(bf16[4096,5,128]{2,0,1:T(8,128)(2,1)} %bitcast.105, bf16[512,5,3,128]{0,3,2,1:T(8,128)(2,1)S(1)} %bitcast.107), kind=kOutput, calls=%fused_computation.1 | convolution fusion | flops 2705323520 | bytes 47851520 | tf_op jit(solution)/shard_map/qhd,khd->hqk/dot_general | solution.py:111
  819.1 17.3 %fusion = f32[5,512]{1,0:T(8,128)S(1)} fusion(f32[5,512,4096]{2,1,0:T(8,128)} %get-tuple-element.47, f32[5,512]{1,0:T(8,128)S(1)} %broadcast_maximum_fusion), kind=kLoop, calls=%fused_computation.2 | loop fusion | flops 31454720 | bytes 41963520 | tf_op jit(solution)/shard_map/reduce_sum | solution.py:115
  836.4 6.0 all-gather.12.cloned.1.call-done
  842.4 17.4 %divide_convert_fusion = bf16[512,5,128]{0,2,1:T(8,128)(2,1)S(1)} fusion(bf16[4096,5,1,128]{0,3,1,2:T(8,128)(2,1)} %all-gather.12.cloned.1.call-done, f32[5,512,4096]{2,1,0:T(8,128)} %get-tuple-element.47, f32[5,512]{1,0:T(8,128)S(1)} %broadcast_maximum_fusion, f32[512,5]{0,1:T(8,128)S(1)} %bitcast.112), kind=kOutput, calls=%fused_computation.82 | convolution fusion | flops 2716467200 | bytes 47861760 | tf_op jit(solution)/shard_map/hqk,khd->hqd/dot_general | solution.py:116
  (70 shorter events, 25.5 us)
Async XLA Ops:
  6.5 178.6 %copy-start = (bf16[768,192]{0,1:T(8,128)(2,1)S(1)}, bf16[768,192]{0,1:T(8,128)(2,1)}, u32[]{:S(2)}) copy-start(bf16[768,192]{0,1:T(8,128)(2,1)} %param.13) | copy-start | bytes 884740
  6.5 10.8 %copy-start.7 = (u32[128]{0:T(128)S(1)}, u32[128]{0:T(128)}, u32[]{:S(2)}) copy-start(u32[128]{0:T(128)} %constant.27) | copy-start | bytes 1540
  6.5 12.0 %copy-start.4 = (bf16[256,320]{0,1:T(8,128)(2,1)S(1)}, bf16[256,320]{0,1:T(8,128)(2,1)}, u32[]{:S(2)}) copy-start(bf16[256,320]{0,1:T(8,128)(2,1)} %param.16) | copy-start | bytes 491524
  6.5 190.2 %all-gather.6.cloned.1.call-start = ((), (), s32[]{:S(2)}) async-start(), calls=%async_computation.1 | async-start | bytes 8110080 | tf_op jit(solution)/shard_map/all_gather | solution.py:87
  7.3 265.3 %all-gather.8.cloned.1.call-start = ((), (), s32[]{:S(2)}) async-start(), calls=%async_computation.2 | async-start | bytes 6553600 | tf_op jit(solution)/shard_map/all_gather | solution.py:92
  8.3 150.8 %copy-start.3 = (bf16[4,16,3072]{2,1,0:T(8,128)(2,1)S(1)}, bf16[4,16,3072]{2,1,0:T(8,128)(2,1)}, u32[]{:S(2)}) copy-start(bf16[4,16,3072]{2,1,0:T(8,128)(2,1)} %param.9) | copy-start | bytes 1179652
  10.8 149.9 %collective-permute-start = (bf16[6,1,32,96]{3,2,1,0:T(8,128)(2,1)}, bf16[6,1,32,96]{3,2,1,0:T(8,128)(2,1)}, u32[]{:S(2)}, u32[]{:S(2)}) collective-permute-start(bf16[6,1,32,96]{3,2,1,0:T(8,128)(2,1)} %get-tuple-element.35), channel_id=1, source_target_pairs={{0,8},{8,16},{16,24},{1,9},{9,17},{17,25},{2,10},{10,18},{18,26},{... | collective-permute-start | bytes 110600 | tf_op jit(solution)/shard_map/ppermute | solution.py:19
  15.3 146.6 %collective-permute-start.1 = (bf16[6,1,32,96]{3,2,1,0:T(8,128)(2,1)}, bf16[6,1,32,96]{3,2,1,0:T(8,128)(2,1)}, u32[]{:S(2)}, u32[]{:S(2)}) collective-permute-start(bf16[6,1,32,96]{3,2,1,0:T(8,128)(2,1)} %get-tuple-element.34), channel_id=1, source_target_pairs={{8,0},{16,8},{24,16},{9,1},{17,9},{25,17},{10,2},{18,10},{26,18},{... | collective-permute-start | bytes 110600 | tf_op jit(solution)/shard_map/ppermute | solution.py:21
  162.9 4.7 collective-permute-start.2
  164.2 6.5 collective-permute-start.3
  169.5 3.4 copy-start.5
  179.2 0.9 copy-start.6
  202.7 2.2 copy-start.2
  204.2 450.2 %all-gather.10.cloned.1.call-start = ((), (), s32[]{:S(2)}) async-start(), calls=%async_computation.3 | async-start | bytes 22118400 | tf_op jit(solution)/shard_map/all_gather | solution.py:96
  208.0 634.4 %all-gather.12.cloned.1.call-start = ((), (), s32[]{:S(2)}) async-start(), calls=%async_computation.4 | async-start | bytes 5898240 | tf_op jit(solution)/shard_map/all_gather | solution.py:109
  842.4 18.5 %copy-start.1 = (bf16[768,192]{0,1:T(8,128)(2,1)S(1)}, bf16[768,192]{0,1:T(8,128)(2,1)}, u32[]{:S(2)}) copy-start(bf16[768,192]{0,1:T(8,128)(2,1)} %param.13) | copy-start | bytes 884740
Sparse Core Ops, SparseCore 0:
  9.0 187.6 all-gather.5
  204.3 68.1 all-gather.7
  274.2 380.1 all-gather.9
  676.0 166.3 all-gather.11
